TPU v7x, 32 devices: a whole 2x2x4 slice. The times are simulated.
32 devices in a mesh: req: 8 (over y, x, core), tp: 4 (over z).
Axes of the slice: x: 2, y: 2, z: 4, core: 2. Of those that a mesh axis runs over, the one named last changes fastest.
Arguments:
- residual: bfloat16 [2048, 2048], P('req', 'tp'), may hold values from -0.29882812 to 0.29882812
- queries: bfloat16 [2048, 1280], P('req', 'tp'), may hold values from -6 to 6
- suffix_kv: bfloat16 [2048, 4, 256], P('req', 'tp'), may hold values from -4 to 4
- prefix_cache: bfloat16 [8192, 4, 256], P('req', 'tp'), may hold values from -6 to 6
- out_weight: bfloat16 [1280, 2048], P('tp'), may hold values from -0.15625 to 0.15625
- norm_gain: bfloat16 [2048], replicated, may hold values from 0.5 to 1.5
- next_query_weight: bfloat16 [2048, 1280], P(None, 'tp'), may hold values from -0.125 to 0.125
- lengths: int32 [8, 4], P('req'), may hold values from 1 to 128, 256 in all within a row
- tenant: int32 [8, 4], P('req'), may hold values from 0 to 3
- owners: int32 [4], replicated, may hold values from 0 to 7, as said below
Outputs:
- new_residual: bfloat16 [2048, 2048], P('req', 'tp')
- next_queries: bfloat16 [2048, 1280], P('req', 'tp')
Inputs may be any that keep to these rules, and one draw needn't show every extreme that they name: `lengths`: each device's 4 requests fill its 256 rows in order. `owners`: distinct.
All inputs are finite; a program needn't handle non-finite values.
Results may differ from a plain program's by a relative error of at most 0.0065.
Values may be sent and summed in bfloat16 or wider, within the bound.
No kernel may reach another device: no remote copies, remote signals or barrier semaphores. Data moves between devices by JAX's collectives and lax.ppermute only.
A program may use at most 64 MiB of HBM per device.

v0:
```python
import jax
import jax.numpy as jnp
from jax import lax
from jax.experimental import pallas as pl
from jax.experimental.pallas import tpu as pltpu
from jax.sharding import PartitionSpec as P

QH = 20
KVH = 5
HD = 64
TENANTS = 4
MOSTLEN = 128
GATHER_SLOTS_MAX = 16


def from_root(block, axis, source):
    block = jnp.where(lax.axis_index(axis) == source, block, jnp.zeros_like(block))
    return lax.psum(block, axis)


def pick_heads(pair_rows, select):
    split_pair = pair_rows.reshape(pair_rows.shape[0], 2, 2, HD)
    key_heads = jnp.einsum(
        "njd,hj->nhd", split_pair[:, :, 0], select, preferred_element_type=jnp.float32
    ).astype(jnp.bfloat16)
    value_heads = jnp.einsum(
        "njd,hj->nhd", split_pair[:, :, 1], select, preferred_element_type=jnp.float32
    ).astype(jnp.bfloat16)
    return (key_heads, value_heads)


def xor_permute(block, mask, n_req):
    pairs = [(source, source ^ mask) for source in range(n_req)]
    return lax.ppermute(block, "req", pairs)


def tenant_slots(own_slot, owners, n_req):
    if n_req <= GATHER_SLOTS_MAX and n_req % 2 == 0 and (n_req & (n_req - 1)) == 0:
        req_index = lax.axis_index("req")
        mine = [own_slot] + [
            xor_permute(own_slot, 2 * chip_mask, n_req) for chip_mask in range(1, n_req // 2)
        ]
        theirs = [xor_permute(block, 1, n_req) for block in mine]
        slots = jnp.concatenate(
            [block for pair in zip(mine, theirs) for block in pair], axis=0
        )
        chip_offset = (owners // 2) ^ (req_index // 2)
        other_core = (owners % 2) != (req_index % 2)
        return slots, 2 * chip_offset + other_core.astype(jnp.int32)
    blocks = [from_root(own_slot, "req", owners[tenant_id]) for tenant_id in range(TENANTS)]
    return jnp.concatenate(blocks, axis=0), jnp.arange(TENANTS, dtype=jnp.int32)


def attention_kernel(
    slot_ref, first_ref, start_ref, query_ref, prefix_ref, suffix_ref, row_ref, pair_ref, out_ref
):
    request = pl.program_id(0)
    first = first_ref[request]
    start = start_ref[request]
    spread = query_ref[...]
    pair_lanes = 2 * HD
    prefix_keys = prefix_ref[:, :pair_lanes]
    prefix_values = prefix_ref[:, pair_lanes:]
    suffix_keys = suffix_ref[:, :pair_lanes]
    suffix_values = suffix_ref[:, pair_lanes:]
    contract = (((1,), (1,)), ((), ()))
    score_scale = HD ** (-0.5)
    prefix_scores = lax.dot_general(
        spread, prefix_keys, contract, preferred_element_type=jnp.float32
    ) * score_scale
    suffix_scores = lax.dot_general(
        spread, suffix_keys, contract, preferred_element_type=jnp.float32
    ) * score_scale
    key_position = first + lax.broadcasted_iota(jnp.int32, suffix_scores.shape, 1)
    query_position = first + row_ref[...]
    allowed = (key_position >= start) & (key_position <= query_position)
    suffix_scores = jnp.where(allowed, suffix_scores, -jnp.inf)
    row_top = jnp.maximum(
        jnp.max(prefix_scores, axis=1, keepdims=True),
        jnp.max(suffix_scores, axis=1, keepdims=True),
    )
    prefix_weights = jnp.exp(prefix_scores - row_top)
    suffix_weights = jnp.where(allowed, jnp.exp(suffix_scores - row_top), 0.0)
    denominator = jnp.sum(prefix_weights, axis=1, keepdims=True) + jnp.sum(
        suffix_weights, axis=1, keepdims=True
    )
    accumulated = jnp.dot(
        prefix_weights.astype(jnp.bfloat16), prefix_values, preferred_element_type=jnp.float32
    ) + jnp.dot(
        suffix_weights.astype(jnp.bfloat16), suffix_values, preferred_element_type=jnp.float32
    )
    attended = accumulated / denominator
    first_pair = attended[:, :HD]
    second_pair = attended[:, HD:]
    picked = jnp.where(pair_ref[...] > 0, second_pair, first_pair).astype(out_ref.dtype)
    window = out_ref.shape[0]
    for head in range(out_ref.shape[1] // HD):
        out_ref[:, head * HD:(head + 1) * HD] = picked[head * window:(head + 1) * window]


def window_attention(
    slot_index, firsts, starts, spread, slots, suffix_windows, query_rows, row_pairs, slot_rows
):
    requests, flat_rows, query_lanes = spread.shape
    window = suffix_windows.shape[1]
    lanes = slots.shape[1]
    head_count = flat_rows // window
    grid_spec = pltpu.PrefetchScalarGridSpec(
        num_scalar_prefetch=3,
        grid=(requests,),
        in_specs=[
            pl.BlockSpec((None, flat_rows, query_lanes), lambda k, slot, first, start: (k, 0, 0)),
            pl.BlockSpec((slot_rows, lanes), lambda k, slot, first, start: (slot[k], 0)),
            pl.BlockSpec((None, window, lanes), lambda k, slot, first, start: (k, 0, 0)),
            pl.BlockSpec((flat_rows, 1), lambda k, slot, first, start: (0, 0)),
            pl.BlockSpec((flat_rows, 1), lambda k, slot, first, start: (0, 0)),
        ],
        out_specs=pl.BlockSpec(
            (None, window, head_count * HD), lambda k, slot, first, start: (k, 0, 0)
        ),
    )
    return pl.pallas_call(
        attention_kernel,
        grid_spec=grid_spec,
        out_shape=jax.ShapeDtypeStruct((requests, window, head_count * HD), jnp.bfloat16),
    )(slot_index, firsts, starts, spread, slots, suffix_windows, query_rows, row_pairs)


def xor_tp(block, mask, n_tp):
    pairs = [(source, source ^ mask) for source in range(n_tp)]
    return lax.ppermute(block, "tp", pairs)


def from_partners(block, n_tp):
    if n_tp == 4:
        near = xor_tp(block, 1, n_tp)
        across = xor_tp(block, 2, n_tp)
        return [block, near, across, xor_tp(across, 1, n_tp)]
    return [block] + [xor_tp(block, mask, n_tp) for mask in range(1, n_tp)]


def shifted(block, shift, n_tp):
    pairs = [(source, (source + shift) % n_tp) for source in range(n_tp)]
    return lax.ppermute(block, "tp", pairs)


def local(
    residual,
    queries,
    suffix_kv,
    prefix_cache,
    out_weight,
    norm_gain,
    next_query_weight,
    lengths,
    tenant,
    owners,
    n_req,
    n_tp,
):
    row_count = queries.shape[0]
    head_count = queries.shape[1] // HD
    width = residual.shape[1]
    tp_index = lax.axis_index("tp")

    weight_pieces = []
    for mask in range(n_tp):
        partner = tp_index ^ mask
        piece = lax.dynamic_slice_in_dim(out_weight, partner * width, width, 1)
        weight_pieces.append(piece if mask == 0 else xor_tp(piece, mask, n_tp))

    head_ids = tp_index * head_count + jnp.arange(head_count, dtype=jnp.int32)
    pair_ids = head_ids // (QH // KVH) - tp_index
    select = (pair_ids[:, None] == jnp.arange(2, dtype=jnp.int32)[None, :]).astype(jnp.bfloat16)
    req_lengths = lengths[0]
    req_tenant = tenant[0]
    req_ends = jnp.cumsum(req_lengths)
    req_starts = req_ends - req_lengths
    position = jnp.arange(row_count, dtype=jnp.int32)
    request_ids = jnp.sum((position[:, None] >= req_ends[None, :]).astype(jnp.int32), axis=1)
    member = request_ids[:, None] == jnp.arange(req_lengths.shape[0], dtype=jnp.int32)[None, :]
    row_start = jnp.sum(jnp.where(member, req_starts[None, :], 0), axis=1)
    row_tenant = jnp.sum(jnp.where(member, req_tenant[None, :], 0), axis=1)
    score_scale = HD ** (-0.5)
    own_slot = jnp.transpose(
        prefix_cache.reshape(prefix_cache.shape[0], 2, 2, HD), (0, 2, 1, 3)
    ).reshape(prefix_cache.shape[0], -1)
    slots, slot_of_tenant = tenant_slots(own_slot, owners, n_req)
    suffix_rows = jnp.transpose(suffix_kv.reshape(row_count, 2, 2, HD), (0, 2, 1, 3)).reshape(
        row_count, -1
    )
    window = min(MOSTLEN, row_count)
    firsts = jnp.minimum(req_starts, row_count - window).astype(jnp.int32)
    head_select = jnp.transpose(select)[:, :, None, None]
    spreads = []
    suffix_windows = []
    for request in range(req_lengths.shape[0]):
        window_queries = lax.dynamic_slice_in_dim(queries, firsts[request], window, 0)
        window_queries = jnp.transpose(window_queries.reshape(window, head_count, HD), (1, 0, 2))
        spread = jnp.concatenate(
            [window_queries * head_select[0], window_queries * head_select[1]], axis=2
        )
        spreads.append(spread.reshape(head_count * window, 2 * HD))
        suffix_windows.append(lax.dynamic_slice_in_dim(suffix_rows, firsts[request], window, 0))
    query_rows = (jnp.arange(head_count * window, dtype=jnp.int32) % window)[:, None]
    row_pairs = jnp.repeat(pair_ids.astype(jnp.int32), window)[:, None]
    slot_index = slot_of_tenant[req_tenant].astype(jnp.int32)
    results = window_attention(
        slot_index,
        firsts,
        req_starts.astype(jnp.int32),
        jnp.stack(spreads),
        slots,
        jnp.stack(suffix_windows),
        query_rows,
        row_pairs,
        own_slot.shape[0],
    )
    attended = jnp.zeros((row_count, head_count * HD), jnp.bfloat16)
    for request in range(req_lengths.shape[0]):
        placed = lax.dynamic_update_slice_in_dim(
            jnp.zeros_like(attended), results[request], firsts[request], 0
        )
        attended = jnp.where((request_ids == request)[:, None], placed, attended)

    head_blocks = from_partners(attended, n_tp)
    projected = None
    for mask in range(n_tp):
        part = jnp.dot(head_blocks[mask], weight_pieces[mask], preferred_element_type=jnp.float32)
        projected = part if projected is None else projected + part
    new_residual = (residual.astype(jnp.float32) + projected).astype(jnp.bfloat16)

    blocks = from_partners(new_residual, n_tp)
    widened = [block.astype(jnp.float32) for block in blocks]
    square_sums = sum(jnp.sum(block * block, axis=1, keepdims=True) for block in widened)
    mean_square = square_sums / (width * n_tp)
    scale = lax.rsqrt(mean_square + 1e-05)
    gain = norm_gain.astype(jnp.float32)
    next_sums = None
    for mask in range(n_tp):
        source = tp_index ^ mask
        block_gain = lax.dynamic_slice_in_dim(gain, source * width, width, 0)
        block_weight = lax.dynamic_slice_in_dim(next_query_weight, source * width, width, 0)
        normed = (widened[mask] * scale * block_gain).astype(jnp.bfloat16)
        part = jnp.dot(normed, block_weight, preferred_element_type=jnp.float32)
        next_sums = part if next_sums is None else next_sums + part
    return (new_residual, next_sums.astype(jnp.bfloat16))


def solution(mesh):
    n_req = mesh.shape["req"]
    n_tp = mesh.shape["tp"]

    def body(*args):
        return local(*args, n_req=n_req, n_tp=n_tp)

    return jax.shard_map(
        body,
        mesh=mesh,
        in_specs=(
            P("req", "tp"),
            P("req", "tp"),
            P("req", "tp", None),
            P("req", "tp", None),
            P("tp", None),
            P(),
            P(None, "tp"),
            P("req", None),
            P("req", None),
            P(),
        ),
        out_specs=(P("req", "tp"), P("req", "tp")),
        check_vma=False,
    )
```

profile of v0, /device:TPU:8, one launch (start us, length us, event | category | flops | bytes accessed | tf_op | source)
XLA Modules:
  0.0 105.9 jit_solution(9922579462130517771)
XLA Ops:
  0.7 1.4 %copy.36 = bf16[1024,1,256]{0,2,1:T(8,128)(2,1)S(1)} copy(bf16[1024,1,256]{2,0,1:T(8,128)(2,1)} %param.13) | data formatting | bytes 1048576 | tf_op args[3]
  2.4 1.6 %collective-permute-start.1 = (bf16[1024,256]{1,0:T(8,128)(2,1)S(1)}, bf16[1024,256]{1,0:T(8,128)(2,1)}, u32[]{:S(2)}, u32[]{:S(2)}) collective-permute-start(bf16[1024,256]{1,0:T(8,128)(2,1)S(1)} %copy.42), channel_id=1, source_target_pairs={{0,8},{4,12},{8,0},{12,4},{16,24},{20,28},{24,16},{28,20},{1,9},{5... | collective-permute-start | bytes 1572872 | tf_op jit(solution)/shard_map/ppermute | solution.py:34
  3.9 1.5 %collective-permute-start.3 = (bf16[1024,256]{1,0:T(8,128)(2,1)S(1)}, bf16[1024,256]{1,0:T(8,128)(2,1)}, u32[]{:S(2)}, u32[]{:S(2)}) collective-permute-start(bf16[1024,256]{1,0:T(8,128)(2,1)S(1)} %copy.42), channel_id=1, source_target_pairs={{0,16},{4,20},{8,24},{12,28},{16,0},{20,4},{24,8},{28,12},{1,17},{... | collective-permute-start | bytes 1572872 | tf_op jit(solution)/shard_map/ppermute | solution.py:34
  5.9 2.1 %constant_dynamic-slice_fusion = (bf16[320,512]{1,0:T(8,128)(2,1)S(1)}, bf16[320,512]{1,0:T(8,128)(2,1)}, bf16[320,512]{1,0:T(8,128)(2,1)}) fusion(bf16[320,2048]{1,0:T(8,128)(2,1)} %param.14, s32[]{:T(128)S(6)} %select_n.131, s32[]{:T(128)S(6)} %select_n.129, s32[]{:T(128)S(6)} %select_n.130), kind=kLoop, calls=%fused_computation.84 | loop fusion | bytes 1966092 | tf_op jit(solution)/shard_map/dynamic_slice | solution.py:169
  8.7 0.6 fusion.47
  15.0 0.6 broadcast_compare_fusion.3
  18.5 0.8 add_select_fusion.row_ref
  19.3 1.0 copy.43
  20.3 0.8 constant_dynamic-slice_fusion.6
  21.4 0.9 copy.46
  22.3 1.6 %copy.45 = bf16[128,256]{1,0:T(8,128)(2,1)} copy(bf16[128,256]{0,1:T(8,128)(2,1)} %get-tuple-element.14) | data formatting | bytes 131072 | tf_op jit(solution)/shard_map/dynamic_slice | solution.py:204
  23.9 0.8 constant_dynamic-update-slice_fusion.7
  24.8 1.6 %pad_maximum_fusion.1.suffix_ref = bf16[4,128,256]{2,1,0:T(8,128)(2,1)} fusion(bf16[1,128,256]{2,1,0:T(8,128)(2,1)S(1)} %bitcast.92, bf16[1,128,256]{2,1,0:T(8,128)(2,1)S(1)} %bitcast.93, bf16[1,128,256]{2,1,0:T(8,128)(2,1)S(1)} %bitcast.94, bf16[1,128,256]{2,1,0:T(8,128)(2,1)} %bitcast.95), kind=kLoop, calls=%fused_computation.43 | loop fusion | flops 393216 | bytes 524288 | tf_op jit(solution)/shard_map/stack | solution.py:214
  27.1 1.0 pad_maximum_fusion.query_ref
  28.0 1.2 %collective-permute-done.3 = bf16[1024,256]{1,0:T(8,128)(2,1)} collective-permute-done((bf16[1024,256]{1,0:T(8,128)(2,1)S(1)}, bf16[1024,256]{1,0:T(8,128)(2,1)}, u32[]{:S(2)}, u32[]{:S(2)}) %collective-permute-start.3) | collective-permute-done | bytes 524320 | tf_op jit(solution)/shard_map/ppermute | solution.py:34
  29.3 0.6 pad_clamp_fusion
  29.9 0.9 copy.51
  30.8 0.7 dynamic-slice.7
  31.5 1.1 %gather_fusion = s32[4]{0:T(128)} fusion(s32[4]{0:T(128)S(1)} %fusion.43, s32[1024]{0:T(1024)S(1)} %pad_clamp_fusion), kind=kCustom, calls=%fused_computation | custom fusion | bytes 48 | tf_op jit(solution)/shard_map/gather | solution.py:207
  32.7 2.6 %collective-permute-start.10 = (bf16[320,512]{1,0:T(8,128)(2,1)}, bf16[320,512]{1,0:T(8,128)(2,1)}, u32[]{:S(2)}, u32[]{:S(2)}) collective-permute-start(bf16[320,512]{1,0:T(8,128)(2,1)} %get-tuple-element.6), channel_id=1, source_target_pairs={{0,2},{1,3},{2,0},{3,1},{4,6},{5,7},{6,4},{7,5},{8,10},{9,11},{10,... | collective-permute-start | bytes 983048 | tf_op jit(solution)/shard_map/ppermute | solution.py:131
  35.5 1.9 %constant_dynamic-update-slice_fusion.6 = bf16[8192,256]{1,0:T(8,128)(2,1)} fusion(bf16[8192,256]{1,0:T(8,128)(2,1)} %constant_dynamic-update-slice_fusion.7, bf16[1024,256]{1,0:T(8,128)(2,1)} %collective-permute-done), kind=kLoop, calls=%fused_computation.76 | loop fusion | bytes 1048576
  37.4 1.9 %constant_dynamic-update-slice_fusion.5 = bf16[8192,256]{1,0:T(8,128)(2,1)} fusion(bf16[8192,256]{1,0:T(8,128)(2,1)} %constant_dynamic-update-slice_fusion.6, bf16[1024,256]{1,0:T(8,128)(2,1)} %collective-permute-done.1), kind=kLoop, calls=%fused_computation.75 | loop fusion | bytes 1048576
  39.2 1.9 %constant_dynamic-update-slice_fusion.4 = bf16[8192,256]{1,0:T(8,128)(2,1)} fusion(bf16[8192,256]{1,0:T(8,128)(2,1)} %constant_dynamic-update-slice_fusion.5, bf16[1024,256]{1,0:T(8,128)(2,1)} %collective-permute-done.2), kind=kLoop, calls=%fused_computation.74 | loop fusion | bytes 1048576
  41.1 1.9 %constant_dynamic-update-slice_fusion.3 = bf16[8192,256]{1,0:T(8,128)(2,1)} fusion(bf16[8192,256]{1,0:T(8,128)(2,1)} %constant_dynamic-update-slice_fusion.4, bf16[1024,256]{1,0:T(8,128)(2,1)} %collective-permute-done.3), kind=kLoop, calls=%fused_computation.73 | loop fusion | bytes 1048576
  43.0 0.8 constant_dynamic-update-slice_fusion.2
  43.8 0.8 constant_dynamic-update-slice_fusion.1
  44.7 0.8 constant_dynamic-update-slice_fusion.prefix_ref
  45.5 10.5 %shard_map.113 = bf16[4,128,320]{2,1,0:T(8,128)(2,1)} custom-call(s32[4]{0:T(128)} %gather_fusion, s32[4]{0:T(128)} %copy-done.4, s32[4]{0:T(128)} %get-tuple-element.3.start_ref, bf16[4,640,128]{2,1,0:T(8,128)(2,1)} %pad_maximum_fusion.query_ref, bf16[8192,256]{1,0:T(8,128)(2,1)} %constant_dynamic-update-slice_fusion.prefix_ref, ...), custom_call_target="tpu_custom_call" | custom-call | tf_op jit(solution)/shard_map/pallas_call | solution.py:122
  56.0 1.1 %slice_bitcast_fusion.1 = (bf16[128,320]{1,0:T(8,128)(2,1)S(1)}, bf16[128,320]{1,0:T(8,128)(2,1)S(1)}, bf16[128,320]{1,0:T(8,128)(2,1)S(1)}) fusion(bf16[4,128,320]{2,1,0:T(8,128)(2,1)} %shard_map.113), kind=kLoop, calls=%fused_computation.59 | loop fusion | bytes 491520 | tf_op jit(solution)/shard_map/squeeze | solution.py:222
  57.1 1.0 fusion.37
  58.1 0.6 dynamic_update_slice.10
  58.7 0.7 dynamic_update_slice.11
  59.4 0.7 dynamic_update_slice.12
  60.1 0.8 select_n.124
  61.1 1.9 %collective-permute-start.7 = (bf16[256,320]{1,0:T(8,128)(2,1)S(1)}, bf16[256,320]{1,0:T(8,128)(2,1)S(1)}, u32[]{:S(2)}, u32[]{:S(2)}) collective-permute-start(bf16[256,320]{1,0:T(8,128)(2,1)S(1)} %select_select_fusion), channel_id=1, source_target_pairs={{0,1},{1,0},{2,3},{3,2},{4,5},{5,4},{6,7},{7,6},{8,9},{9,8},{10,11... | collective-permute-start | bytes 491528 | tf_op jit(solution)/shard_map/ppermute | solution.py:131
  63.0 1.7 %collective-permute-start.9 = (bf16[256,320]{1,0:T(8,128)(2,1)S(1)}, bf16[256,320]{1,0:T(8,128)(2,1)S(1)}, u32[]{:S(2)}, u32[]{:S(2)}) collective-permute-start(bf16[256,320]{1,0:T(8,128)(2,1)S(1)} %select_select_fusion), channel_id=1, source_target_pairs={{0,2},{1,3},{2,0},{3,1},{4,6},{5,7},{6,4},{7,5},{8,10},{9,11},{10,... | collective-permute-start | bytes 491528 | tf_op jit(solution)/shard_map/ppermute | solution.py:131
  64.7 1.3 %fusion.20 = f32[256,512]{1,0:T(8,128)S(1)} fusion(bf16[256,320]{1,0:T(8,128)(2,1)S(1)} %select_select_fusion, bf16[320,2048]{1,0:T(8,128)(2,1)} %param.14, s32[]{:T(128)S(6)} %select_n.128), kind=kOutput, calls=%fused_computation.37 | convolution fusion | flops 83886080 | bytes 1015812 | tf_op jit(solution)/shard_map/dot_general | solution.py:229
  66.0 8.6 %collective-permute-done.9 = bf16[256,320]{1,0:T(8,128)(2,1)S(1)} collective-permute-done((bf16[256,320]{1,0:T(8,128)(2,1)S(1)}, bf16[256,320]{1,0:T(8,128)(2,1)S(1)}, u32[]{:S(2)}, u32[]{:S(2)}) %collective-permute-start.9) | collective-permute-done | bytes 163872 | tf_op jit(solution)/shard_map/ppermute | solution.py:131
  74.5 1.7 %collective-permute-start.11 = (bf16[256,320]{1,0:T(8,128)(2,1)S(1)}, bf16[256,320]{1,0:T(8,128)(2,1)S(1)}, u32[]{:S(2)}, u32[]{:S(2)}) collective-permute-start(bf16[256,320]{1,0:T(8,128)(2,1)S(1)} %collective-permute-done.9), channel_id=1, source_target_pairs={{0,1},{1,0},{2,3},{3,2},{4,5},{5,4},{6,7},{7,6},{8,9},{9,8},{10,11... | collective-permute-start | bytes 491528 | tf_op jit(solution)/shard_map/ppermute | solution.py:131
  76.2 1.3 %convolution_add_fusion.2 = f32[256,512]{1,0:T(8,128)S(1)} fusion(f32[256,512]{1,0:T(8,128)S(1)} %fusion.20, bf16[256,320]{1,0:T(8,128)(2,1)S(1)} %collective-permute-done.7, bf16[320,512]{1,0:T(8,128)(2,1)} %collective-permute-done.8), kind=kOutput, calls=%fused_computation.4 | convolution fusion | flops 84017152 | bytes 1540096 | tf_op jit(solution)/shard_map/dot_general | solution.py:229
  77.5 1.3 %convolution_add_fusion.1 = f32[256,512]{1,0:T(8,128)S(1)} fusion(f32[256,512]{1,0:T(8,128)S(1)} %convolution_add_fusion.2, bf16[256,320]{1,0:T(8,128)(2,1)S(1)} %collective-permute-done.9, bf16[320,512]{1,0:T(8,128)(2,1)} %collective-permute-done.10), kind=kOutput, calls=%fused_computation.3 | convolution fusion | flops 84017152 | bytes 1540096 | tf_op jit(solution)/shard_map/dot_general | solution.py:229
  78.8 2.4 %collective-permute-done.11 = bf16[256,320]{1,0:T(8,128)(2,1)S(1)} collective-permute-done((bf16[256,320]{1,0:T(8,128)(2,1)S(1)}, bf16[256,320]{1,0:T(8,128)(2,1)S(1)}, u32[]{:S(2)}, u32[]{:S(2)}) %collective-permute-start.11) | collective-permute-done | bytes 163872 | tf_op jit(solution)/shard_map/ppermute | solution.py:131
  81.2 1.4 %fusion.3 = (f32[256]{0:T(256)S(1)}, bf16[256,512]{1,0:T(8,128)(2,1)S(1)}) fusion(f32[256,512]{1,0:T(8,128)S(1)} %convolution_add_fusion.1, bf16[256,320]{1,0:T(8,128)(2,1)S(1)} %collective-permute-done.11, bf16[320,512]{1,0:T(8,128)(2,1)} %collective-permute-done.12, bf16[256,512]{1,0:T(8,128)(2,1)S(1)} %copy-done.3), kind=kOutput, calls=%fused_computation.19 | convolution fusion | flops 84803328 | bytes 1541120 | tf_op jit(solution)/shard_map/dot_general | solution.py:229
  82.5 2.6 %collective-permute-start.14 = (bf16[256,512]{1,0:T(8,128)(2,1)S(1)}, bf16[256,512]{1,0:T(8,128)(2,1)S(1)}, u32[]{:S(2)}, u32[]{:S(2)}) collective-permute-start(bf16[256,512]{1,0:T(8,128)(2,1)S(1)} %get-tuple-element.47), channel_id=1, source_target_pairs={{0,2},{1,3},{2,0},{3,1},{4,6},{5,7},{6,4},{7,5},{8,10},{9,11},{10,... | collective-permute-start | bytes 786440 | tf_op jit(solution)/shard_map/ppermute | solution.py:131
  85.5 9.9 %collective-permute-done.14 = bf16[256,512]{1,0:T(8,128)(2,1)S(1)} collective-permute-done((bf16[256,512]{1,0:T(8,128)(2,1)S(1)}, bf16[256,512]{1,0:T(8,128)(2,1)S(1)}, u32[]{:S(2)}, u32[]{:S(2)}) %collective-permute-start.14) | collective-permute-done | bytes 262176 | tf_op jit(solution)/shard_map/ppermute | solution.py:131
  95.4 1.4 %collective-permute-start.15 = (bf16[256,512]{1,0:T(8,128)(2,1)S(1)}, bf16[256,512]{1,0:T(8,128)(2,1)S(1)}, u32[]{:S(2)}, u32[]{:S(2)}) collective-permute-start(bf16[256,512]{1,0:T(8,128)(2,1)S(1)} %collective-permute-done.14), channel_id=1, source_target_pairs={{0,1},{1,0},{2,3},{3,2},{4,5},{5,4},{6,7},{7,6},{8,9},{9,8},{10,11... | collective-permute-start | bytes 786440 | tf_op jit(solution)/shard_map/ppermute | solution.py:131
  97.2 6.4 %collective-permute-done.15 = bf16[256,512]{1,0:T(8,128)(2,1)S(1)} collective-permute-done((bf16[256,512]{1,0:T(8,128)(2,1)S(1)}, bf16[256,512]{1,0:T(8,128)(2,1)S(1)}, u32[]{:S(2)}, u32[]{:S(2)}) %collective-permute-start.15) | collective-permute-done | bytes 262176 | tf_op jit(solution)/shard_map/ppermute | solution.py:131
  104.8 1.0 fusion.2
  (77 shorter events, 5.9 us)
Async XLA Ops:
  0.6 103.1 %copy-start = (bf16[2048,320]{0,1:T(8,128)(2,1)S(1)}, bf16[2048,320]{0,1:T(8,128)(2,1)}, u32[]{:S(2)}) copy-start(bf16[2048,320]{0,1:T(8,128)(2,1)} %param.16) | copy-start | bytes 3932164
  0.6 7.4 %copy-start.8 = (s32[1,4]{1,0:T(1,128)S(1)}, s32[1,4]{1,0:T(1,128)}, u32[]{:S(2)}) copy-start(s32[1,4]{1,0:T(1,128)} %param.17) | copy-start | bytes 52
  0.7 13.8 %copy-start.10 = (s32[1,4]{1,0:T(1,128)S(1)}, s32[1,4]{1,0:T(1,128)}, u32[]{:S(2)}) copy-start(s32[1,4]{1,0:T(1,128)} %param.18) | copy-start | bytes 52
  0.7 17.5 %copy-start.9 = (s32[4]{0:T(128)S(1)}, s32[4]{0:T(128)}, u32[]{:S(2)}) copy-start(s32[4]{0:T(128)} %param.19) | copy-start | bytes 52
  0.7 17.5 %copy-start.2 = (bf16[256,320]{0,1:T(8,128)(2,1)S(1)}, bf16[256,320]{0,1:T(8,128)(2,1)}, u32[]{:S(2)}) copy-start(bf16[256,320]{0,1:T(8,128)(2,1)} %param.11) | copy-start | bytes 491524
  2.3 30.4 %collective-permute-start = (bf16[1024,256]{1,0:T(8,128)(2,1)S(1)}, bf16[1024,256]{1,0:T(8,128)(2,1)}, u32[]{:S(2)}, u32[]{:S(2)}) collective-permute-start(bf16[1024,256]{1,0:T(8,128)(2,1)S(1)} %copy.42), channel_id=1, source_target_pairs={{0,4},{4,0},{8,12},{12,8},{16,20},{20,16},{24,28},{28,24},{1,5},{5... | collective-permute-start | bytes 1572872 | tf_op jit(solution)/shard_map/ppermute | solution.py:34
  2.4 22.4 %collective-permute-start.1 = (bf16[1024,256]{1,0:T(8,128)(2,1)S(1)}, bf16[1024,256]{1,0:T(8,128)(2,1)}, u32[]{:S(2)}, u32[]{:S(2)}) collective-permute-start(bf16[1024,256]{1,0:T(8,128)(2,1)S(1)} %copy.42), channel_id=1, source_target_pairs={{0,8},{4,12},{8,0},{12,4},{16,24},{20,28},{24,16},{28,20},{1,9},{5... | collective-permute-start | bytes 1572872 | tf_op jit(solution)/shard_map/ppermute | solution.py:34
  3.9 25.3 %collective-permute-start.3 = (bf16[1024,256]{1,0:T(8,128)(2,1)S(1)}, bf16[1024,256]{1,0:T(8,128)(2,1)}, u32[]{:S(2)}, u32[]{:S(2)}) collective-permute-start(bf16[1024,256]{1,0:T(8,128)(2,1)S(1)} %copy.42), channel_id=1, source_target_pairs={{0,16},{4,20},{8,24},{12,28},{16,0},{20,4},{24,8},{28,12},{1,17},{... | collective-permute-start | bytes 1572872 | tf_op jit(solution)/shard_map/ppermute | solution.py:34
  5.5 29.8 %collective-permute-start.5 = (bf16[1024,256]{1,0:T(8,128)(2,1)S(1)}, bf16[1024,256]{1,0:T(8,128)(2,1)S(1)}, u32[]{:S(2)}, u32[]{:S(2)}) collective-permute-start(bf16[1024,256]{1,0:T(8,128)(2,1)S(1)} %copy.42), channel_id=1, source_target_pairs={{0,24},{4,28},{8,16},{12,20},{16,8},{20,12},{24,0},{28,4},{1,25},{... | collective-permute-start | bytes 1572872 | tf_op jit(solution)/shard_map/ppermute | solution.py:34
  8.0 68.2 %collective-permute-start.8 = (bf16[320,512]{1,0:T(8,128)(2,1)}, bf16[320,512]{1,0:T(8,128)(2,1)}, u32[]{:S(2)}, u32[]{:S(2)}) collective-permute-start(bf16[320,512]{1,0:T(8,128)(2,1)} %get-tuple-element.5), channel_id=1, source_target_pairs={{0,1},{1,0},{2,3},{3,2},{4,5},{5,4},{6,7},{7,6},{8,9},{9,8},{10,11... | collective-permute-start | bytes 983048 | tf_op jit(solution)/shard_map/ppermute | solution.py:131
  8.7 19.3 %copy-start.4 = (s32[4]{0:T(128)}, s32[4]{0:T(128)S(1)}, u32[]{:S(2)}) copy-start(s32[4]{0:T(128)S(1)} %get-tuple-element.2.first_ref) | copy-start | bytes 52
  24.8 14.5 %collective-permute-start.2 = (bf16[1024,256]{1,0:T(8,128)(2,1)}, bf16[1024,256]{1,0:T(8,128)(2,1)}, u32[]{:S(2)}, u32[]{:S(2)}) collective-permute-start(bf16[1024,256]{1,0:T(8,128)(2,1)} %collective-permute-done.1), channel_id=1, source_target_pairs={{0,4},{4,0},{8,12},{12,8},{16,20},{20,16},{24,28},{28,24},{1,5},{5... | collective-permute-start | bytes 1572872 | tf_op jit(solution)/shard_map/ppermute | solution.py:34
  29.3 13.7 %collective-permute-start.4 = (bf16[1024,256]{1,0:T(8,128)(2,1)}, bf16[1024,256]{1,0:T(8,128)(2,1)S(1)}, u32[]{:S(2)}, u32[]{:S(2)}) collective-permute-start(bf16[1024,256]{1,0:T(8,128)(2,1)} %collective-permute-done.3), channel_id=1, source_target_pairs={{0,4},{4,0},{8,12},{12,8},{16,20},{20,16},{24,28},{28,24},{1,5},{5... | collective-permute-start | bytes 1572872 | tf_op jit(solution)/shard_map/ppermute | solution.py:34
  32.7 44.8 %collective-permute-start.10 = (bf16[320,512]{1,0:T(8,128)(2,1)}, bf16[320,512]{1,0:T(8,128)(2,1)}, u32[]{:S(2)}, u32[]{:S(2)}) collective-permute-start(bf16[320,512]{1,0:T(8,128)(2,1)} %get-tuple-element.6), channel_id=1, source_target_pairs={{0,2},{1,3},{2,0},{3,1},{4,6},{5,7},{6,4},{7,5},{8,10},{9,11},{10,... | collective-permute-start | bytes 983048 | tf_op jit(solution)/shard_map/ppermute | solution.py:131
  35.3 9.4 %collective-permute-start.6 = (bf16[1024,256]{1,0:T(8,128)(2,1)S(1)}, bf16[1024,256]{1,0:T(8,128)(2,1)S(1)}, u32[]{:S(2)}, u32[]{:S(2)}) collective-permute-start(bf16[1024,256]{1,0:T(8,128)(2,1)S(1)} %collective-permute-done.5), channel_id=1, source_target_pairs={{0,4},{4,0},{8,12},{12,8},{16,20},{20,16},{24,28},{28,24},{1,5},{5... | collective-permute-start | bytes 1572872 | tf_op jit(solution)/shard_map/ppermute | solution.py:34
  39.2 39.5 %collective-permute-start.12 = (bf16[320,512]{1,0:T(8,128)(2,1)S(1)}, bf16[320,512]{1,0:T(8,128)(2,1)}, u32[]{:S(2)}, u32[]{:S(2)}) collective-permute-start(bf16[320,512]{1,0:T(8,128)(2,1)S(1)} %get-tuple-element.4), channel_id=1, source_target_pairs={{0,3},{1,2},{2,1},{3,0},{4,7},{5,6},{6,5},{7,4},{8,11},{9,10},{10,... | collective-permute-start | bytes 983048 | tf_op jit(solution)/shard_map/ppermute | solution.py:131
  45.5 15.4 %copy-start.6 = (pred[256]{0:T(512)(128)(4,1)S(1)}, pred[256]{0:T(512)(128)(4,1)}, u32[]{:S(2)}) copy-start(pred[256]{0:T(512)(128)(4,1)} %get-tuple-element.38) | copy-start | bytes 772
  45.5 15.4 %copy-start.7 = (pred[256]{0:T(512)(128)(4,1)S(1)}, pred[256]{0:T(512)(128)(4,1)}, u32[]{:S(2)}) copy-start(pred[256]{0:T(512)(128)(4,1)} %get-tuple-element.39) | copy-start | bytes 772
  56.0 25.2 %copy-start.3 = (bf16[256,512]{1,0:T(8,128)(2,1)S(1)}, bf16[256,512]{1,0:T(8,128)(2,1)}, u32[]{:S(2)}) copy-start(bf16[256,512]{1,0:T(8,128)(2,1)} %param.10) | copy-start | bytes 786436
  58.0 38.8 %copy-start.5 = (bf16[2048]{0:T(1024)(128)(2,1)S(1)}, bf16[2048]{0:T(1024)(128)(2,1)}, u32[]{:S(2)}) copy-start(bf16[2048]{0:T(1024)(128)(2,1)} %param.15) | copy-start | bytes 12292
  61.1 15.1 %collective-permute-start.7 = (bf16[256,320]{1,0:T(8,128)(2,1)S(1)}, bf16[256,320]{1,0:T(8,128)(2,1)S(1)}, u32[]{:S(2)}, u32[]{:S(2)}) collective-permute-start(bf16[256,320]{1,0:T(8,128)(2,1)S(1)} %select_select_fusion), channel_id=1, source_target_pairs={{0,1},{1,0},{2,3},{3,2},{4,5},{5,4},{6,7},{7,6},{8,9},{9,8},{10,11... | collective-permute-start | bytes 491528 | tf_op jit(solution)/shard_map/ppermute | solution.py:131
  63.0 11.5 %collective-permute-start.9 = (bf16[256,320]{1,0:T(8,128)(2,1)S(1)}, bf16[256,320]{1,0:T(8,128)(2,1)S(1)}, u32[]{:S(2)}, u32[]{:S(2)}) collective-permute-start(bf16[256,320]{1,0:T(8,128)(2,1)S(1)} %select_select_fusion), channel_id=1, source_target_pairs={{0,2},{1,3},{2,0},{3,1},{4,6},{5,7},{6,4},{7,5},{8,10},{9,11},{10,... | collective-permute-start | bytes 491528 | tf_op jit(solution)/shard_map/ppermute | solution.py:131
  74.5 6.6 %collective-permute-start.11 = (bf16[256,320]{1,0:T(8,128)(2,1)S(1)}, bf16[256,320]{1,0:T(8,128)(2,1)S(1)}, u32[]{:S(2)}, u32[]{:S(2)}) collective-permute-start(bf16[256,320]{1,0:T(8,128)(2,1)S(1)} %collective-permute-done.9), channel_id=1, source_target_pairs={{0,1},{1,0},{2,3},{3,2},{4,5},{5,4},{6,7},{7,6},{8,9},{9,8},{10,11... | collective-permute-start | bytes 491528 | tf_op jit(solution)/shard_map/ppermute | solution.py:131
  82.5 23.3 %copy-start.1 = (bf16[256,512]{1,0:T(8,128)(2,1)}, bf16[256,512]{1,0:T(8,128)(2,1)S(1)}, u32[]{:S(2)}) copy-start(bf16[256,512]{1,0:T(8,128)(2,1)S(1)} %get-tuple-element.47) | copy-start | bytes 786436
  82.5 12.9 %collective-permute-start.14 = (bf16[256,512]{1,0:T(8,128)(2,1)S(1)}, bf16[256,512]{1,0:T(8,128)(2,1)S(1)}, u32[]{:S(2)}, u32[]{:S(2)}) collective-permute-start(bf16[256,512]{1,0:T(8,128)(2,1)S(1)} %get-tuple-element.47), channel_id=1, source_target_pairs={{0,2},{1,3},{2,0},{3,1},{4,6},{5,7},{6,4},{7,5},{8,10},{9,11},{10,... | collective-permute-start | bytes 786440 | tf_op jit(solution)/shard_map/ppermute | solution.py:131
  85.2 11.9 %collective-permute-start.13 = (bf16[256,512]{1,0:T(8,128)(2,1)S(1)}, bf16[256,512]{1,0:T(8,128)(2,1)S(1)}, u32[]{:S(2)}, u32[]{:S(2)}) collective-permute-start(bf16[256,512]{1,0:T(8,128)(2,1)S(1)} %get-tuple-element.47), channel_id=1, source_target_pairs={{0,1},{1,0},{2,3},{3,2},{4,5},{5,4},{6,7},{7,6},{8,9},{9,8},{10,11... | collective-permute-start | bytes 786440 | tf_op jit(solution)/shard_map/ppermute | solution.py:131
  95.4 8.2 %collective-permute-start.15 = (bf16[256,512]{1,0:T(8,128)(2,1)S(1)}, bf16[256,512]{1,0:T(8,128)(2,1)S(1)}, u32[]{:S(2)}, u32[]{:S(2)}) collective-permute-start(bf16[256,512]{1,0:T(8,128)(2,1)S(1)} %collective-permute-done.14), channel_id=1, source_target_pairs={{0,1},{1,0},{2,3},{3,2},{4,5},{5,4},{6,7},{7,6},{8,9},{9,8},{10,11... | collective-permute-start | bytes 786440 | tf_op jit(solution)/shard_map/ppermute | solution.py:131
where the time goes:
time: 108 us; the launch traced here: 106 us
  waiting for transfers between devices  28.5 us (26%)
  local copies, waits for them, and re-layouts  27.5 us (25%)
  starting transfers between devices  16.1 us (15%)
  Pallas kernels  10.5 us (10%)
  between operations  8.54 us (8%)
  other arithmetic  7.5 us (7%)
  matrix products  7.27 us (7%)
    ppermute x9, waiting for transfers between devices, xor_tp(): return lax.ppermute(block, 'tp', pairs)  27.3 us
    unnamed x34, local copies, waits for them, and re-layouts  13.4 us
    ppermute x9, starting transfers between devices, xor_tp(): return lax.ppermute(block, 'tp', pairs)  12.2 us
    pallas_call x1, Pallas kernels, window_attention(): pl.pallas_call(attention_kernel, grid_spec=grid_spec, out_shape=jax.Shape...  10.5 us
    dot_general x4, matrix products, local(): jnp.dot(head_blocks[mask], weight_pieces[mask], preferred_element_type=jn...  5.17 us
    ppermute x7, starting transfers between devices, xor_permute(): return lax.ppermute(block, 'req', pairs)  3.86 us
    dynamic_slice x5, local copies, waits for them, and re-layouts, local(): lax.dynamic_slice_in_dim(suffix_rows, firsts[request], window, 0)  3.54 us
  transfers between devices with their start and end apart: 16, of which 5 were waited for; matrix products, arithmetic and copies ran while one was open for 35% of the time, Pallas kernels for 10%

commit v1 on v0

--- a/solution.py
+++ b/solution.py
@@ -64,13 +64,12 @@
     suffix_keys = suffix_ref[:, :pair_lanes]
     suffix_values = suffix_ref[:, pair_lanes:]
     contract = (((1,), (1,)), ((), ()))
-    score_scale = HD ** (-0.5)
     prefix_scores = lax.dot_general(
         spread, prefix_keys, contract, preferred_element_type=jnp.float32
-    ) * score_scale
+    )
     suffix_scores = lax.dot_general(
         spread, suffix_keys, contract, preferred_element_type=jnp.float32
-    ) * score_scale
+    )
     key_position = first + lax.broadcasted_iota(jnp.int32, suffix_scores.shape, 1)
     query_position = first + row_ref[...]
     allowed = (key_position >= start) & (key_position <= query_position)
@@ -80,7 +79,7 @@
         jnp.max(suffix_scores, axis=1, keepdims=True),
     )
     prefix_weights = jnp.exp(prefix_scores - row_top)
-    suffix_weights = jnp.where(allowed, jnp.exp(suffix_scores - row_top), 0.0)
+    suffix_weights = jnp.exp(suffix_scores - row_top)
     denominator = jnp.sum(prefix_weights, axis=1, keepdims=True) + jnp.sum(
         suffix_weights, axis=1, keepdims=True
     )
@@ -200,7 +199,7 @@
         spread = jnp.concatenate(
             [window_queries * head_select[0], window_queries * head_select[1]], axis=2
         )
-        spreads.append(spread.reshape(head_count * window, 2 * HD))
+        spreads.append((spread * score_scale).reshape(head_count * window, 2 * HD))
         suffix_windows.append(lax.dynamic_slice_in_dim(suffix_rows, firsts[request], window, 0))
     query_rows = (jnp.arange(head_count * window, dtype=jnp.int32) % window)[:, None]
     row_pairs = jnp.repeat(pair_ids.astype(jnp.int32), window)[:, None]
@@ -215,13 +214,9 @@
         query_rows,
         row_pairs,
         own_slot.shape[0],
-    )
-    attended = jnp.zeros((row_count, head_count * HD), jnp.bfloat16)
-    for request in range(req_lengths.shape[0]):
-        placed = lax.dynamic_update_slice_in_dim(
-            jnp.zeros_like(attended), results[request], firsts[request], 0
-        )
-        attended = jnp.where((request_ids == request)[:, None], placed, attended)
+    ).reshape(-1, head_count * HD)
+    source_rows = request_ids * window + position - firsts[request_ids]
+    attended = jnp.take(results, source_rows, axis=0)
 
     head_blocks = from_partners(attended, n_tp)
     projected = None

time: 108 us -> 106 us (0.981)
  the two profiles are of different devices: /device:TPU:8 before, /device:TPU:0 now
where the time goes in v1:
time: 106 us; the launch traced here: 105 us
  waiting for transfers between devices  29.8 us (28%)
  local copies, waits for them, and re-layouts  22.2 us (21%)
  starting transfers between devices  20.4 us (19%)
  Pallas kernels  10 us (9%)
  other arithmetic  9.2 us (9%)
  between operations  8.41 us (8%)
  matrix products  5.32 us (5%)
    ppermute x9, waiting for transfers between devices, xor_tp(): return lax.ppermute(block, 'tp', pairs)  29.7 us
    ppermute x9, starting transfers between devices, xor_tp(): return lax.ppermute(block, 'tp', pairs)  15.3 us
    unnamed x36, local copies, waits for them, and re-layouts  12.5 us
    pallas_call x1, Pallas kernels, window_attention(): pl.pallas_call(attention_kernel, grid_spec=grid_spec, out_shape=jax.Shape...  10 us
    ppermute x7, starting transfers between devices, xor_permute(): return lax.ppermute(block, 'req', pairs)  5.06 us
    dot_general x4, matrix products, local(): jnp.dot(head_blocks[mask], weight_pieces[mask], preferred_element_type=jn...  3.22 us
    select_n x2, other arithmetic, local(): attended = jnp.take(results, source_rows, axis=0)  3.18 us
    gather x1, local copies, waits for them, and re-layouts, local(): attended = jnp.take(results, source_rows, axis=0)  2.23 us
  transfers between devices with their start and end apart: 16, of which 5 were waited for; matrix products, arithmetic and copies ran while one was open for 31% of the time, Pallas kernels for 10%

profile of v1, /device:TPU:0, one launch (start us, length us, event | category | flops | bytes accessed | tf_op | source)
XLA Modules:
  0.0 105.3 jit_solution(7247659976819591508)
XLA Ops:
  0.7 1.4 %copy.44 = bf16[1024,1,256]{0,2,1:T(8,128)(2,1)S(1)} copy(bf16[1024,1,256]{2,0,1:T(8,128)(2,1)} %param.13) | data formatting | bytes 1048576 | tf_op args[3]
  2.3 0.5 collective-permute-start
  2.8 2.6 %collective-permute-start.1 = (bf16[1024,256]{1,0:T(8,128)(2,1)S(1)}, bf16[1024,256]{1,0:T(8,128)(2,1)}, u32[]{:S(2)}, u32[]{:S(2)}) collective-permute-start(bf16[1024,256]{1,0:T(8,128)(2,1)S(1)} %copy.50), channel_id=1, source_target_pairs={{0,8},{4,12},{8,0},{12,4},{16,24},{20,28},{24,16},{28,20},{1,9},{5... | collective-permute-start | bytes 1572872 | tf_op jit(solution)/shard_map/ppermute | solution.py:34
  5.4 1.5 %collective-permute-start.3 = (bf16[1024,256]{1,0:T(8,128)(2,1)S(1)}, bf16[1024,256]{1,0:T(8,128)(2,1)}, u32[]{:S(2)}, u32[]{:S(2)}) collective-permute-start(bf16[1024,256]{1,0:T(8,128)(2,1)S(1)} %copy.50), channel_id=1, source_target_pairs={{0,16},{4,20},{8,24},{12,28},{16,0},{20,4},{24,8},{28,12},{1,17},{... | collective-permute-start | bytes 1572872 | tf_op jit(solution)/shard_map/ppermute | solution.py:34
  6.9 2.2 %constant_dynamic-slice_fusion = (bf16[320,512]{1,0:T(8,128)(2,1)}, bf16[320,512]{1,0:T(8,128)(2,1)}, bf16[320,512]{1,0:T(8,128)(2,1)}) fusion(bf16[320,2048]{1,0:T(8,128)(2,1)} %param.14, s32[]{:T(128)S(6)} %select_n.138, s32[]{:T(128)S(6)} %select_n.136, s32[]{:T(128)S(6)} %select_n.137), kind=kLoop, calls=%fused_computation.83 | loop fusion | bytes 1966092 | tf_op jit(solution)/shard_map/dynamic_slice | solution.py:168
  9.1 2.0 %collective-permute-start.8 = (bf16[320,512]{1,0:T(8,128)(2,1)}, bf16[320,512]{1,0:T(8,128)(2,1)}, u32[]{:S(2)}, u32[]{:S(2)}) collective-permute-start(bf16[320,512]{1,0:T(8,128)(2,1)} %get-tuple-element.7), channel_id=1, source_target_pairs={{0,1},{1,0},{2,3},{3,2},{4,5},{5,4},{6,7},{7,6},{8,9},{9,8},{10,11... | collective-permute-start | bytes 983048 | tf_op jit(solution)/shard_map/ppermute | solution.py:130
  11.3 0.5 broadcast_minimum_fusion
  11.9 0.6 fusion.46
  17.4 0.8 add_select_fusion.row_ref
  21.9 3.1 %compare_select_fusion = (s32[256,1]{0,1:T(1,128)}, s32[256,1]{0,1:T(1,128)S(1)}) fusion(s32[256,1]{0,1:T(1,128)S(1)} %bitcast.101, s32[]{:T(128)} %bitcast.7, s32[]{:T(128)} %bitcast.6, s32[]{:T(128)} %bitcast.5, s32[]{:T(128)} %bitcast.4), kind=kLoop, calls=%fused_computation.74 | loop fusion | flops 3840 | bytes 3088 | tf_op jit(solution)/shard_map/jit(_take)/jit(_where)/select_n | solution.py:219
  25.0 0.5 compare_and_fusion
  27.5 0.7 pad_maximum_fusion.1.suffix_ref
  28.2 0.8 constant_dynamic-update-slice_fusion.7
  29.1 0.6 pad_clamp_fusion.1
  29.7 0.9 pad_maximum_fusion.query_ref
  30.7 0.4 collective-permute-start.4
  31.2 0.7 pad_clamp_fusion
  31.8 0.9 copy.59
  32.8 1.3 %gather_fusion = s32[4]{0:T(128)} fusion(s32[4]{0:T(128)S(1)} %fusion.42, s32[1024]{0:T(1024)} %pad_clamp_fusion.1), kind=kCustom, calls=%fused_computation | custom fusion | bytes 48 | tf_op jit(solution)/shard_map/gather | solution.py:206
  34.0 2.6 %collective-permute-start.10 = (bf16[320,512]{1,0:T(8,128)(2,1)}, bf16[320,512]{1,0:T(8,128)(2,1)S(1)}, u32[]{:S(2)}, u32[]{:S(2)}) collective-permute-start(bf16[320,512]{1,0:T(8,128)(2,1)} %get-tuple-element.8), channel_id=1, source_target_pairs={{0,2},{1,3},{2,0},{3,1},{4,6},{5,7},{6,4},{7,5},{8,10},{9,11},{10,... | collective-permute-start | bytes 983048 | tf_op jit(solution)/shard_map/ppermute | solution.py:130
  36.6 1.9 %constant_dynamic-update-slice_fusion.6 = bf16[8192,256]{1,0:T(8,128)(2,1)} fusion(bf16[8192,256]{1,0:T(8,128)(2,1)} %constant_dynamic-update-slice_fusion.7, bf16[1024,256]{1,0:T(8,128)(2,1)} %collective-permute-done), kind=kLoop, calls=%fused_computation.72 | loop fusion | bytes 1048576
  38.5 1.9 %constant_dynamic-update-slice_fusion.5 = bf16[8192,256]{1,0:T(8,128)(2,1)} fusion(bf16[8192,256]{1,0:T(8,128)(2,1)} %constant_dynamic-update-slice_fusion.6, bf16[1024,256]{1,0:T(8,128)(2,1)} %collective-permute-done.1), kind=kLoop, calls=%fused_computation.71 | loop fusion | bytes 1048576
  40.4 1.2 %collective-permute-start.12 = (bf16[320,512]{1,0:T(8,128)(2,1)S(1)}, bf16[320,512]{1,0:T(8,128)(2,1)S(1)}, u32[]{:S(2)}, u32[]{:S(2)}) collective-permute-start(bf16[320,512]{1,0:T(8,128)(2,1)S(1)} %copy-done.3), channel_id=1, source_target_pairs={{0,3},{1,2},{2,1},{3,0},{4,7},{5,6},{6,5},{7,4},{8,11},{9,10},{10,... | collective-permute-start | bytes 983048 | tf_op jit(solution)/shard_map/ppermute | solution.py:130
  41.5 0.8 constant_dynamic-update-slice_fusion.4
  42.4 1.9 %constant_dynamic-update-slice_fusion.3 = bf16[8192,256]{1,0:T(8,128)(2,1)} fusion(bf16[8192,256]{1,0:T(8,128)(2,1)} %constant_dynamic-update-slice_fusion.4, bf16[1024,256]{1,0:T(8,128)(2,1)} %collective-permute-done.3), kind=kLoop, calls=%fused_computation.69 | loop fusion | bytes 1048576
  44.2 0.8 constant_dynamic-update-slice_fusion.2
  45.1 1.9 %constant_dynamic-update-slice_fusion.1 = bf16[8192,256]{1,0:T(8,128)(2,1)} fusion(bf16[8192,256]{1,0:T(8,128)(2,1)} %constant_dynamic-update-slice_fusion.2, bf16[1024,256]{1,0:T(8,128)(2,1)} %collective-permute-done.5), kind=kLoop, calls=%fused_computation.67 | loop fusion | bytes 1048576
  46.9 0.8 constant_dynamic-update-slice_fusion.prefix_ref
  47.8 10.0 %shard_map.113 = bf16[4,128,320]{2,1,0:T(8,128)(2,1)} custom-call(s32[4]{0:T(128)} %gather_fusion, s32[4]{0:T(128)} %copy-done.6, s32[4]{0:T(128)} %get-tuple-element.5.start_ref, bf16[4,640,128]{2,1,0:T(8,128)(2,1)} %pad_maximum_fusion.query_ref, bf16[8192,256]{1,0:T(8,128)(2,1)} %constant_dynamic-update-slice_fusion.prefix_ref, ...), custom_call_target="tpu_custom_call" | custom-call | tf_op jit(solution)/shard_map/pallas_call | solution.py:121
  57.8 2.2 %gather_fusion.1 = bf16[256,320]{1,0:T(8,128)(2,1)S(1)} fusion(bf16[512,320]{1,0:T(8,128)(2,1)} %bitcast.77, s32[1024]{0:T(1024)S(1)} %pad_clamp_fusion), kind=kCustom, calls=%fused_computation.1 | custom fusion | bytes 328704 | tf_op jit(solution)/shard_map/jit(_take)/gather | solution.py:219
  60.2 0.3 collective-permute-start.7
  60.5 3.0 %collective-permute-start.9 = (bf16[256,320]{1,0:T(8,128)(2,1)S(1)}, bf16[256,320]{1,0:T(8,128)(2,1)S(1)}, u32[]{:S(2)}, u32[]{:S(2)}) collective-permute-start(bf16[256,320]{1,0:T(8,128)(2,1)S(1)} %broadcast_select_fusion), channel_id=1, source_target_pairs={{0,2},{1,3},{2,0},{3,1},{4,6},{5,7},{6,4},{7,5},{8,10},{9,11},{10,... | collective-permute-start | bytes 491528 | tf_op jit(solution)/shard_map/ppermute | solution.py:130
  63.5 1.3 %fusion.20 = f32[256,512]{1,0:T(8,128)S(1)} fusion(bf16[256,320]{1,0:T(8,128)(2,1)S(1)} %broadcast_select_fusion, bf16[320,2048]{1,0:T(8,128)(2,1)} %param.14, s32[]{:T(128)S(6)} %select_n.135), kind=kOutput, calls=%fused_computation.38 | convolution fusion | flops 83886080 | bytes 1015812 | tf_op jit(solution)/shard_map/dot_general | solution.py:224
  64.7 9.6 %collective-permute-done.9 = bf16[256,320]{1,0:T(8,128)(2,1)S(1)} collective-permute-done((bf16[256,320]{1,0:T(8,128)(2,1)S(1)}, bf16[256,320]{1,0:T(8,128)(2,1)S(1)}, u32[]{:S(2)}, u32[]{:S(2)}) %collective-permute-start.9) | collective-permute-done | bytes 163872 | tf_op jit(solution)/shard_map/ppermute | solution.py:130
  74.3 0.7 collective-permute-start.11
  75.0 1.3 %convolution_add_fusion.2 = f32[256,512]{1,0:T(8,128)S(1)} fusion(f32[256,512]{1,0:T(8,128)S(1)} %fusion.20, bf16[256,320]{1,0:T(8,128)(2,1)S(1)} %collective-permute-done.7, bf16[320,512]{1,0:T(8,128)(2,1)} %collective-permute-done.8), kind=kOutput, calls=%fused_computation.5 | convolution fusion | flops 84017152 | bytes 1540096 | tf_op jit(solution)/shard_map/dot_general | solution.py:224
  76.3 0.3 convolution_add_fusion.1
  76.6 3.8 %collective-permute-done.11 = bf16[256,320]{1,0:T(8,128)(2,1)S(1)} collective-permute-done((bf16[256,320]{1,0:T(8,128)(2,1)S(1)}, bf16[256,320]{1,0:T(8,128)(2,1)S(1)}, u32[]{:S(2)}, u32[]{:S(2)}) %collective-permute-start.11) | collective-permute-done | bytes 163872 | tf_op jit(solution)/shard_map/ppermute | solution.py:130
  80.4 0.4 fusion.3
  80.8 3.2 %collective-permute-start.14 = (bf16[256,512]{1,0:T(8,128)(2,1)S(1)}, bf16[256,512]{1,0:T(8,128)(2,1)S(1)}, u32[]{:S(2)}, u32[]{:S(2)}) collective-permute-start(bf16[256,512]{1,0:T(8,128)(2,1)S(1)} %get-tuple-element.42), channel_id=1, source_target_pairs={{0,2},{1,3},{2,0},{3,1},{4,6},{5,7},{6,4},{7,5},{8,10},{9,11},{10,... | collective-permute-start | bytes 786440 | tf_op jit(solution)/shard_map/ppermute | solution.py:130
  84.0 1.7 %collective-permute-start.13 = (bf16[256,512]{1,0:T(8,128)(2,1)S(1)}, bf16[256,512]{1,0:T(8,128)(2,1)S(1)}, u32[]{:S(2)}, u32[]{:S(2)}) collective-permute-start(bf16[256,512]{1,0:T(8,128)(2,1)S(1)} %get-tuple-element.42), channel_id=1, source_target_pairs={{0,1},{1,0},{2,3},{3,2},{4,5},{5,4},{6,7},{7,6},{8,9},{9,8},{10,11... | collective-permute-start | bytes 786440 | tf_op jit(solution)/shard_map/ppermute | solution.py:130
  85.8 10.0 %collective-permute-done.14 = bf16[256,512]{1,0:T(8,128)(2,1)S(1)} collective-permute-done((bf16[256,512]{1,0:T(8,128)(2,1)S(1)}, bf16[256,512]{1,0:T(8,128)(2,1)S(1)}, u32[]{:S(2)}, u32[]{:S(2)}) %collective-permute-start.14) | collective-permute-done | bytes 262176 | tf_op jit(solution)/shard_map/ppermute | solution.py:130
  95.7 0.6 collective-permute-start.15
  96.7 6.3 %collective-permute-done.15 = bf16[256,512]{1,0:T(8,128)(2,1)S(1)} collective-permute-done((bf16[256,512]{1,0:T(8,128)(2,1)S(1)}, bf16[256,512]{1,0:T(8,128)(2,1)S(1)}, u32[]{:S(2)}, u32[]{:S(2)}) %collective-permute-start.15) | collective-permute-done | bytes 262176 | tf_op jit(solution)/shard_map/ppermute | solution.py:130
  103.2 0.4 fusion.18
  103.6 0.4 convolution_add_fusion.5
  103.9 0.4 convolution_add_fusion.4
  104.3 1.0 fusion.2
  (75 shorter events, 4.3 us)
Async XLA Ops:
  0.6 102.5 %copy-start = (bf16[2048,320]{0,1:T(8,128)(2,1)S(1)}, bf16[2048,320]{0,1:T(8,128)(2,1)}, u32[]{:S(2)}) copy-start(bf16[2048,320]{0,1:T(8,128)(2,1)} %param.16) | copy-start | bytes 3932164
  0.6 10.5 %copy-start.9 = (s32[1,4]{1,0:T(1,128)S(1)}, s32[1,4]{1,0:T(1,128)}, u32[]{:S(2)}) copy-start(s32[1,4]{1,0:T(1,128)} %param.17) | copy-start | bytes 52
  0.7 17.6 %copy-start.11 = (s32[1,4]{1,0:T(1,128)S(1)}, s32[1,4]{1,0:T(1,128)}, u32[]{:S(2)}) copy-start(s32[1,4]{1,0:T(1,128)} %param.18) | copy-start | bytes 52
  0.7 20.1 %copy-start.2 = (bf16[256,320]{0,1:T(8,128)(2,1)S(1)}, bf16[256,320]{0,1:T(8,128)(2,1)}, u32[]{:S(2)}) copy-start(bf16[256,320]{0,1:T(8,128)(2,1)} %param.11) | copy-start | bytes 491524
  0.7 24.9 %copy-start.10 = (s32[4]{0:T(128)S(1)}, s32[4]{0:T(128)}, u32[]{:S(2)}) copy-start(s32[4]{0:T(128)} %param.19) | copy-start | bytes 52
  2.1 24.4 %copy-start.5 = (bf16[256,1,256]{2,0,1:T(8,128)(2,1)S(1)}, bf16[256,1,256]{2,0,1:T(8,128)(2,1)}, u32[]{:S(2)}) copy-start(bf16[256,1,256]{2,0,1:T(8,128)(2,1)} %param.12) | copy-start | bytes 393220
  2.3 31.7 %collective-permute-start = (bf16[1024,256]{1,0:T(8,128)(2,1)S(1)}, bf16[1024,256]{1,0:T(8,128)(2,1)}, u32[]{:S(2)}, u32[]{:S(2)}) collective-permute-start(bf16[1024,256]{1,0:T(8,128)(2,1)S(1)} %copy.50), channel_id=1, source_target_pairs={{0,4},{4,0},{8,12},{12,8},{16,20},{20,16},{24,28},{28,24},{1,5},{5... | collective-permute-start | bytes 1572872 | tf_op jit(solution)/shard_map/ppermute | solution.py:34
  2.8 26.3 %collective-permute-start.1 = (bf16[1024,256]{1,0:T(8,128)(2,1)S(1)}, bf16[1024,256]{1,0:T(8,128)(2,1)}, u32[]{:S(2)}, u32[]{:S(2)}) collective-permute-start(bf16[1024,256]{1,0:T(8,128)(2,1)S(1)} %copy.50), channel_id=1, source_target_pairs={{0,8},{4,12},{8,0},{12,4},{16,24},{20,28},{24,16},{28,20},{1,9},{5... | collective-permute-start | bytes 1572872 | tf_op jit(solution)/shard_map/ppermute | solution.py:34
  5.4 25.3 %collective-permute-start.3 = (bf16[1024,256]{1,0:T(8,128)(2,1)S(1)}, bf16[1024,256]{1,0:T(8,128)(2,1)}, u32[]{:S(2)}, u32[]{:S(2)}) collective-permute-start(bf16[1024,256]{1,0:T(8,128)(2,1)S(1)} %copy.50), channel_id=1, source_target_pairs={{0,16},{4,20},{8,24},{12,28},{16,0},{20,4},{24,8},{28,12},{1,17},{... | collective-permute-start | bytes 1572872 | tf_op jit(solution)/shard_map/ppermute | solution.py:34
  6.9 29.7 %collective-permute-start.5 = (bf16[1024,256]{1,0:T(8,128)(2,1)S(1)}, bf16[1024,256]{1,0:T(8,128)(2,1)}, u32[]{:S(2)}, u32[]{:S(2)}) collective-permute-start(bf16[1024,256]{1,0:T(8,128)(2,1)S(1)} %copy.50), channel_id=1, source_target_pairs={{0,24},{4,28},{8,16},{12,20},{16,8},{20,12},{24,0},{28,4},{1,25},{... | collective-permute-start | bytes 1572872 | tf_op jit(solution)/shard_map/ppermute | solution.py:34
  9.1 65.9 %collective-permute-start.8 = (bf16[320,512]{1,0:T(8,128)(2,1)}, bf16[320,512]{1,0:T(8,128)(2,1)}, u32[]{:S(2)}, u32[]{:S(2)}) collective-permute-start(bf16[320,512]{1,0:T(8,128)(2,1)} %get-tuple-element.7), channel_id=1, source_target_pairs={{0,1},{1,0},{2,3},{3,2},{4,5},{5,4},{6,7},{7,6},{8,9},{9,8},{10,11... | collective-permute-start | bytes 983048 | tf_op jit(solution)/shard_map/ppermute | solution.py:130
  11.9 17.2 %copy-start.6 = (s32[4]{0:T(128)}, s32[4]{0:T(128)S(1)}, u32[]{:S(2)}) copy-start(s32[4]{0:T(128)S(1)} %get-tuple-element.4.first_ref) | copy-start | bytes 52
  26.5 13.8 %copy-start.3 = (bf16[320,512]{1,0:T(8,128)(2,1)S(1)}, bf16[320,512]{1,0:T(8,128)(2,1)}, u32[]{:S(2)}) copy-start(bf16[320,512]{1,0:T(8,128)(2,1)} %get-tuple-element.6) | copy-start | bytes 983044
  29.1 11.3 %collective-permute-start.2 = (bf16[1024,256]{1,0:T(8,128)(2,1)}, bf16[1024,256]{1,0:T(8,128)(2,1)S(1)}, u32[]{:S(2)}, u32[]{:S(2)}) collective-permute-start(bf16[1024,256]{1,0:T(8,128)(2,1)} %collective-permute-done.1), channel_id=1, source_target_pairs={{0,4},{4,0},{8,12},{12,8},{16,20},{20,16},{24,28},{28,24},{1,5},{5... | collective-permute-start | bytes 1572872 | tf_op jit(solution)/shard_map/ppermute | solution.py:34
  30.7 13.5 %collective-permute-start.4 = (bf16[1024,256]{1,0:T(8,128)(2,1)}, bf16[1024,256]{1,0:T(8,128)(2,1)S(1)}, u32[]{:S(2)}, u32[]{:S(2)}) collective-permute-start(bf16[1024,256]{1,0:T(8,128)(2,1)} %collective-permute-done.3), channel_id=1, source_target_pairs={{0,4},{4,0},{8,12},{12,8},{16,20},{20,16},{24,28},{28,24},{1,5},{5... | collective-permute-start | bytes 1572872 | tf_op jit(solution)/shard_map/ppermute | solution.py:34
  34.0 42.3 %collective-permute-start.10 = (bf16[320,512]{1,0:T(8,128)(2,1)}, bf16[320,512]{1,0:T(8,128)(2,1)S(1)}, u32[]{:S(2)}, u32[]{:S(2)}) collective-permute-start(bf16[320,512]{1,0:T(8,128)(2,1)} %get-tuple-element.8), channel_id=1, source_target_pairs={{0,2},{1,3},{2,0},{3,1},{4,6},{5,7},{6,4},{7,5},{8,10},{9,11},{10,... | collective-permute-start | bytes 983048 | tf_op jit(solution)/shard_map/ppermute | solution.py:130
  36.6 10.3 %collective-permute-start.6 = (bf16[1024,256]{1,0:T(8,128)(2,1)}, bf16[1024,256]{1,0:T(8,128)(2,1)S(1)}, u32[]{:S(2)}, u32[]{:S(2)}) collective-permute-start(bf16[1024,256]{1,0:T(8,128)(2,1)} %collective-permute-done.5), channel_id=1, source_target_pairs={{0,4},{4,0},{8,12},{12,8},{16,20},{20,16},{24,28},{28,24},{1,5},{5... | collective-permute-start | bytes 1572872 | tf_op jit(solution)/shard_map/ppermute | solution.py:34
  40.4 36.2 %collective-permute-start.12 = (bf16[320,512]{1,0:T(8,128)(2,1)S(1)}, bf16[320,512]{1,0:T(8,128)(2,1)S(1)}, u32[]{:S(2)}, u32[]{:S(2)}) collective-permute-start(bf16[320,512]{1,0:T(8,128)(2,1)S(1)} %copy-done.3), channel_id=1, source_target_pairs={{0,3},{1,2},{2,1},{3,0},{4,7},{5,6},{6,5},{7,4},{8,11},{9,10},{10,... | collective-permute-start | bytes 983048 | tf_op jit(solution)/shard_map/ppermute | solution.py:130
  47.8 12.3 %copy-start.8 = (pred[256]{0:T(512)(128)(4,1)S(1)}, pred[256]{0:T(512)(128)(4,1)}, u32[]{:S(2)}) copy-start(pred[256]{0:T(512)(128)(4,1)} %compare_and_fusion) | copy-start | bytes 772
  57.8 22.6 %copy-start.4 = (bf16[256,512]{1,0:T(8,128)(2,1)S(1)}, bf16[256,512]{1,0:T(8,128)(2,1)}, u32[]{:S(2)}) copy-start(bf16[256,512]{1,0:T(8,128)(2,1)} %param.10) | copy-start | bytes 786436
  57.8 38.5 %copy-start.7 = (bf16[2048]{0:T(1024)(128)(2,1)S(1)}, bf16[2048]{0:T(1024)(128)(2,1)}, u32[]{:S(2)}) copy-start(bf16[2048]{0:T(1024)(128)(2,1)} %param.15) | copy-start | bytes 12292
  60.2 14.9 %collective-permute-start.7 = (bf16[256,320]{1,0:T(8,128)(2,1)S(1)}, bf16[256,320]{1,0:T(8,128)(2,1)S(1)}, u32[]{:S(2)}, u32[]{:S(2)}) collective-permute-start(bf16[256,320]{1,0:T(8,128)(2,1)S(1)} %broadcast_select_fusion), channel_id=1, source_target_pairs={{0,1},{1,0},{2,3},{3,2},{4,5},{5,4},{6,7},{7,6},{8,9},{9,8},{10,11... | collective-permute-start | bytes 491528 | tf_op jit(solution)/shard_map/ppermute | solution.py:130
  60.5 13.9 %collective-permute-start.9 = (bf16[256,320]{1,0:T(8,128)(2,1)S(1)}, bf16[256,320]{1,0:T(8,128)(2,1)S(1)}, u32[]{:S(2)}, u32[]{:S(2)}) collective-permute-start(bf16[256,320]{1,0:T(8,128)(2,1)S(1)} %broadcast_select_fusion), channel_id=1, source_target_pairs={{0,2},{1,3},{2,0},{3,1},{4,6},{5,7},{6,4},{7,5},{8,10},{9,11},{10,... | collective-permute-start | bytes 491528 | tf_op jit(solution)/shard_map/ppermute | solution.py:130
  74.3 6.0 %collective-permute-start.11 = (bf16[256,320]{1,0:T(8,128)(2,1)S(1)}, bf16[256,320]{1,0:T(8,128)(2,1)S(1)}, u32[]{:S(2)}, u32[]{:S(2)}) collective-permute-start(bf16[256,320]{1,0:T(8,128)(2,1)S(1)} %collective-permute-done.9), channel_id=1, source_target_pairs={{0,1},{1,0},{2,3},{3,2},{4,5},{5,4},{6,7},{7,6},{8,9},{9,8},{10,11... | collective-permute-start | bytes 491528 | tf_op jit(solution)/shard_map/ppermute | solution.py:130
  80.8 24.5 %copy-start.1 = (bf16[256,512]{1,0:T(8,128)(2,1)}, bf16[256,512]{1,0:T(8,128)(2,1)S(1)}, u32[]{:S(2)}) copy-start(bf16[256,512]{1,0:T(8,128)(2,1)S(1)} %get-tuple-element.42) | copy-start | bytes 786436
  80.8 15.0 %collective-permute-start.14 = (bf16[256,512]{1,0:T(8,128)(2,1)S(1)}, bf16[256,512]{1,0:T(8,128)(2,1)S(1)}, u32[]{:S(2)}, u32[]{:S(2)}) collective-permute-start(bf16[256,512]{1,0:T(8,128)(2,1)S(1)} %get-tuple-element.42), channel_id=1, source_target_pairs={{0,2},{1,3},{2,0},{3,1},{4,6},{5,7},{6,4},{7,5},{8,10},{9,11},{10,... | collective-permute-start | bytes 786440 | tf_op jit(solution)/shard_map/ppermute | solution.py:130
  84.0 12.5 %collective-permute-start.13 = (bf16[256,512]{1,0:T(8,128)(2,1)S(1)}, bf16[256,512]{1,0:T(8,128)(2,1)S(1)}, u32[]{:S(2)}, u32[]{:S(2)}) collective-permute-start(bf16[256,512]{1,0:T(8,128)(2,1)S(1)} %get-tuple-element.42), channel_id=1, source_target_pairs={{0,1},{1,0},{2,3},{3,2},{4,5},{5,4},{6,7},{7,6},{8,9},{9,8},{10,11... | collective-permute-start | bytes 786440 | tf_op jit(solution)/shard_map/ppermute | solution.py:130
  95.7 7.3 %collective-permute-start.15 = (bf16[256,512]{1,0:T(8,128)(2,1)S(1)}, bf16[256,512]{1,0:T(8,128)(2,1)S(1)}, u32[]{:S(2)}, u32[]{:S(2)}) collective-permute-start(bf16[256,512]{1,0:T(8,128)(2,1)S(1)} %collective-permute-done.14), channel_id=1, source_target_pairs={{0,1},{1,0},{2,3},{3,2},{4,5},{5,4},{6,7},{7,6},{8,9},{9,8},{10,11... | collective-permute-start | bytes 786440 | tf_op jit(solution)/shard_map/ppermute | solution.py:130
